TPU v7x, 256 devices: a whole 4x4x8 slice. The times are simulated.
256 devices in a mesh: role: 2 (over core), dp: 16 (over x, y), tensor: 8 (over z).
Axes of the slice: x: 4, y: 4, z: 8, core: 2. Of those that a mesh axis runs over, the one named last changes fastest.
Arguments:
- queries: bfloat16 [1024, 128, 576], P(('dp', 'tensor'), 'role'), may hold values from -13 to 13
- latent_cache: bfloat16 [512, 1024, 576], P(('dp', 'tensor')), may hold values from -4 to 4
- new_latent: bfloat16 [1024, 576], P(('dp', 'tensor')), may hold values from -9 to 9
- cache_lengths: int32 [512], P(('dp', 'tensor')), may hold values from 2 to 1024
- value_proj: bfloat16 [128, 512, 128], P(('role', 'tensor')), may hold values from -1 to 1
- out_proj: bfloat16 [16384, 7168], P(('role', 'tensor'), 'dp'), may hold values from -0.046875 to 0.046875
- residual: bfloat16 [1024, 7168], P(('role', 'tensor'), 'dp'), may hold values from -68 to 68
- norm_gain: bfloat16 [7168], replicated, may hold values from 0.5 to 1.5
- routes: int32 [1024, 8], P(('role', 'tensor')), may hold values from 0 to 15, all different within a row; in each aligned block of 64 rows (0 to 63, 64 to 127, ...) at most 40 rows name the same one
- gate_values: float32 [1024, 8], P(('role', 'tensor')), may hold values from 0.2 to 0.8
- tenant_ids: int32 [1024], P(('role', 'tensor')), may hold values from 0 to 2
- expert_gate_weight: bfloat16 [16, 7168, 2048], P('dp', None, ('role', 'tensor')), may hold values from -0.0625 to 0.0625
- expert_up_weight: bfloat16 [16, 7168, 2048], P('dp', None, ('role', 'tensor')), may hold values from -0.0625 to 0.0625
- expert_down_weight: bfloat16 [16, 2048, 7168], P('dp', ('role', 'tensor')), may hold values from -0.125 to 0.125
- left_delta_factor: bfloat16 [3, 16, 2048, 64], P(None, 'dp', ('role', 'tensor')), may hold values from -0.125 to 0.125
- factor_right: bfloat16 [3, 16, 64, 7168], P(None, 'dp'), may hold values from -0.75 to 0.75
Outputs:
- mixed: bfloat16 [1024, 7168], P(('role', 'tensor'), 'dp')
Inputs may be any that keep to these rules, and one draw needn't show every extreme that they name: `routes`: in each aligned block of 64 tokens no expert is named by more than 40 of them.
All inputs are finite; a program needn't handle non-finite values.
Results may differ from a plain program's by a relative error of at most 0.008.
Values may be sent and summed in bfloat16 or wider, within the bound.
No kernel may reach another device: no remote copies, remote signals or barrier semaphores. Data moves between devices by JAX's collectives and lax.ppermute only.
A program may use at most 128 MiB of HBM per device.

v0:
```python
import jax
import jax.numpy as jnp
from jax import lax
from jax.sharding import PartitionSpec as P

LAT = 512
EXPERTS = 16
TEN = 3
SCORE_SCALE = 0.07216878364870323
NORM_EPS = 1e-06
MASKED = -1e30
RT = ("role", "tensor")


def rms_rows(input_rows, norm_gain):
    wide = input_rows.astype(jnp.float32)
    scale = lax.rsqrt(jnp.mean(wide * wide, axis=-1, keepdims=True) + NORM_EPS)
    return (wide * scale * norm_gain.astype(jnp.float32)).astype(jnp.bfloat16)


def slot_table(routes, expert, capacity):
    hit = jnp.any(routes == expert, axis=-1).astype(jnp.int32)
    earlier = jnp.cumsum(hit, axis=-1) - hit
    slot_ids = jnp.arange(capacity, dtype=jnp.int32)
    return (hit[..., None, :] > 0) & (earlier[..., None, :] == slot_ids[:, None])


def local(
    queries,
    latent_cache,
    new_latent,
    cache_lengths,
    value_proj,
    out_proj,
    residual,
    norm_gain,
    routes,
    gate_values,
    tenant_ids,
    expert_gate_weight,
    expert_up_weight,
    expert_down_weight,
    left_delta_factor,
    factor_right,
):
    n_slices = lax.axis_size(RT)
    slice_idx = lax.axis_index(RT)
    group_rows = residual.shape[0]
    capacity = 5 * group_rows // 8
    model_width = expert_down_weight.shape[2]
    col_width = model_width // n_slices
    expert = lax.axis_index("dp")
    labels = jnp.arange(EXPERTS, dtype=jnp.int32)
    table = slot_table(routes, labels[:, None, None], capacity)
    mine = lax.dynamic_index_in_dim(table, expert, 0, keepdims=False)
    mine_owner = jnp.sum(mine.astype(jnp.int32) * tenant_ids[None, :], axis=1)
    hidden_slice = expert_down_weight.shape[1]
    down_local = expert_down_weight[0].reshape(hidden_slice, n_slices, col_width)
    left_local = left_delta_factor[:, 0]
    tenants, _, rank = left_local.shape
    left_local = jnp.transpose(left_local, (1, 0, 2)).reshape(hidden_slice, 1, tenants * rank)
    left_local = jnp.broadcast_to(left_local, (hidden_slice, n_slices, tenants * rank))
    down_pack = jnp.concatenate([down_local, left_local], axis=2)
    pack_width = down_pack.shape[2]
    slot_token = jnp.sum(
        mine.astype(jnp.int32) * jnp.arange(group_rows, dtype=jnp.int32)[None, :], axis=1
    )
    slot_used = jnp.sum(mine.astype(jnp.int32), axis=1)
    info = jnp.concatenate([slot_token, slot_used, mine_owner]).astype(jnp.bfloat16)
    info_rows = jnp.zeros((8, pack_width), jnp.bfloat16).at[0, : info.shape[0]].set(info)
    info_rows = jnp.broadcast_to(info_rows[:, None, :], (8, n_slices, pack_width))
    down_pack = jnp.concatenate([down_pack, info_rows], axis=0)
    down_pack = lax.all_to_all(down_pack, RT, split_axis=1, concat_axis=0, tiled=True)
    right_w = lax.dynamic_slice_in_dim(factor_right[:, 0], slice_idx * col_width, col_width, 2)
    seq_count, context, width = latent_cache.shape
    local_heads = queries.shape[1]
    paired = queries.reshape(seq_count, 2, local_heads, width)
    scores = (
        jnp.einsum("sqhd,spd->sqhp", paired, latent_cache, preferred_element_type=jnp.float32)
        * SCORE_SCALE
    )
    present = jnp.arange(context, dtype=jnp.int32)[None, :] < cache_lengths[:, None]
    scores = jnp.where(present[:, None, None, :], scores, MASKED)
    fresh_keys = new_latent.reshape(seq_count, 2, width)
    fresh = (
        jnp.einsum("sqhd,skd->sqhk", paired, fresh_keys, preferred_element_type=jnp.float32)
        * SCORE_SCALE
    )
    causal = jnp.arange(2)[:, None] >= jnp.arange(2)[None, :]
    fresh = jnp.where(causal[None, :, None, :], fresh, MASKED)
    top = jnp.maximum(jnp.max(scores, axis=3), jnp.max(fresh, axis=3))[..., None]
    weights = jnp.exp(scores - top)
    fresh_weights = jnp.exp(fresh - top)
    total = jnp.sum(weights, axis=3) + jnp.sum(fresh_weights, axis=3)
    summed = jnp.einsum(
        "sqhp,spd->sqhd",
        weights.astype(jnp.bfloat16),
        latent_cache[:, :, :LAT],
        preferred_element_type=jnp.float32,
    )
    summed = summed + jnp.einsum(
        "sqhk,skd->sqhd",
        fresh_weights.astype(jnp.bfloat16),
        fresh_keys[:, :, :LAT],
        preferred_element_type=jnp.float32,
    )
    attended = (
        (summed / total[..., None]).astype(jnp.bfloat16).reshape(seq_count * 2, local_heads, LAT)
    )
    by_head = lax.all_to_all(attended, "tensor", split_axis=1, concat_axis=0, tiled=True)
    head_values = jnp.einsum(
        "thl,hlv->thv", by_head, value_proj, preferred_element_type=jnp.float32
    ).astype(jnp.bfloat16)
    head_values = head_values.reshape(
        head_values.shape[0], head_values.shape[1] * head_values.shape[2]
    )
    all_values = lax.all_gather(head_values, "dp", axis=0, tiled=True)
    down_pack, all_values = lax.optimization_barrier((down_pack, all_values))
    partial = jnp.dot(all_values, out_proj, preferred_element_type=jnp.float32)
    partial = lax.psum_scatter(partial, "role", scatter_dimension=0, tiled=True)
    attention = lax.psum_scatter(partial, "tensor", scatter_dimension=0, tiled=True)
    mixed_in = lax.optimization_barrier(
        (residual.astype(jnp.float32) + attention).astype(jnp.bfloat16)
    )
    down_pack = down_pack.reshape(n_slices, hidden_slice + 8, pack_width)
    info = down_pack[:, hidden_slice, : 3 * capacity].astype(jnp.int32)
    slot_token, slot_used, owners = (
        info[:, :capacity],
        info[:, capacity : 2 * capacity],
        info[:, 2 * capacity :],
    )
    owners = owners.reshape(n_slices * capacity)
    n_cols = lax.axis_size("dp")
    everything = lax.all_gather(mixed_in, ("role", "tensor", "dp"), axis=0, tiled=True)
    everything = everything.reshape(n_slices, n_cols, group_rows, mixed_in.shape[1])
    one_hot = (slot_token[:, :, None] == jnp.arange(group_rows, dtype=jnp.int32)[None, None, :]) & (
        slot_used[:, :, None] > 0
    )
    picked = jnp.einsum(
        "ncg,ndgk->ncdk",
        one_hot.astype(jnp.bfloat16),
        everything,
        preferred_element_type=jnp.float32,
    )
    picked = picked.reshape(n_slices * capacity, model_width)
    scale = lax.rsqrt(jnp.mean(picked * picked, axis=-1, keepdims=True) + NORM_EPS)
    collected_rows = (picked * scale * norm_gain.astype(jnp.float32)).astype(jnp.bfloat16)
    gate_scores = jnp.dot(collected_rows, expert_gate_weight[0], preferred_element_type=jnp.float32)
    upper_bound = jnp.dot(collected_rows, expert_up_weight[0], preferred_element_type=jnp.float32)
    hidden = (jax.nn.silu(gate_scores) * upper_bound).astype(jnp.bfloat16)
    gathered = lax.all_gather(hidden, RT, axis=0, tiled=False)
    hidden_all = jnp.transpose(gathered, (1, 0, 2)).reshape(hidden.shape[0], -1)
    down_pack = down_pack[:, :hidden_slice].reshape(n_slices * hidden_slice, pack_width)
    down_w = down_pack[:, :col_width]
    left_w = down_pack[:, col_width:].reshape(n_slices * hidden_slice, tenants, rank)
    base_output = jnp.dot(hidden_all, down_w, preferred_element_type=jnp.float32)
    owner_mask = (owners[:, None] == jnp.arange(TEN, dtype=jnp.int32)[None, :]).astype(jnp.float32)
    mixing = (
        jnp.einsum("sf,ftr->str", hidden_all, left_w, preferred_element_type=jnp.float32)
        * owner_mask[:, :, None]
    )
    delta = jnp.einsum(
        "str,trd->sd", mixing, right_w.astype(jnp.float32), precision=lax.Precision.HIGHEST
    )
    expert_out = (base_output - delta).astype(jnp.bfloat16)
    expert_out = expert_out.reshape(n_slices, capacity, col_width)
    by_group = lax.all_to_all(expert_out, RT, split_axis=0, concat_axis=0, tiled=True)
    by_expert = lax.all_to_all(by_group, "dp", split_axis=0, concat_axis=0, tiled=True)
    chosen = (routes[:, :, None] == labels[None, None, :]).astype(jnp.float32)
    gate_of = jnp.sum(gate_values[:, :, None] * chosen, axis=1)
    weighting = table.astype(jnp.float32) * gate_of.T[:, None, :]
    expert_part = jnp.einsum(
        "ecg,ecd->gd", weighting, by_expert.astype(jnp.float32), precision=lax.Precision.HIGHEST
    )
    return (mixed_in.astype(jnp.float32) + expert_part).astype(jnp.bfloat16)


def solution(mesh):
    placed = (
        P(("dp", "tensor"), "role", None),
        P(("dp", "tensor"), None, None),
        P(("dp", "tensor"), None),
        P(("dp", "tensor")),
        P(("role", "tensor"), None, None),
        P(("role", "tensor"), "dp"),
        P(("role", "tensor"), "dp"),
        P(),
        P(("role", "tensor"), None),
        P(("role", "tensor"), None),
        P(("role", "tensor")),
        P("dp", None, ("role", "tensor")),
        P("dp", None, ("role", "tensor")),
        P("dp", ("role", "tensor"), None),
        P(None, "dp", ("role", "tensor"), None),
        P(None, "dp", None, None),
    )
    return jax.shard_map(
        local, mesh=mesh, in_specs=placed, out_specs=P(("role", "tensor"), "dp"), check_vma=False
    )
```

profile of v0, /device:TPU:32, one launch (start us, length us, event | category | flops | bytes accessed | tf_op | source)
XLA Modules:
  0.0 471.5 jit_solution(3004877601197552970)
XLA Ops:
  8.9 1.7 fusion.64
  10.5 3.8 fusion.7
  15.0 1.7 fusion.2
  18.3 8.7 %all-to-all-start.1 = ((bf16[8,64,512]{2,0,1:T(8,128)(2,1)}), bf16[8,64,512]{2,0,1:T(8,128)(2,1)S(1)}, u32[]{:S(2)}, u32[]{:S(2)}) async-start(bf16[8,64,512]{2,0,1:T(8,128)(2,1)} %copy.65), calls=%async_computation.1 | async-start | bytes 1048576 | tf_op jit(solution)/shard_map/all_to_all | solution.py:110
  27.7 3.9 copy.61
  33.1 3.5 pad_maximum_fusion
  36.6 6.2 %copy.63 = bf16[136,16,640]{2,0,1:T(8,128)(2,1)} copy(bf16[136,16,640]{0,2,1:T(8,128)(2,1)} %pad_maximum_fusion) | data formatting | bytes 5570560 | tf_op jit(solution)/shard_map/concatenate | solution.py:72
  43.0 7.0 %all-to-all-start = ((bf16[136,16,640]{2,0,1:T(8,128)(2,1)}), bf16[136,16,640]{2,0,1:T(8,128)(2,1)}, u32[]{:S(2)}, u32[]{:S(2)}) async-start(bf16[136,16,640]{2,0,1:T(8,128)(2,1)} %copy.63), calls=%async_computation | async-start | bytes 5570560 | tf_op jit(solution)/shard_map/all_to_all | solution.py:73
  50.1 1.5 fusion.25
  52.4 52.1 %all-gather.5.cloned.1.call-done = bf16[1024,1024]{1,0:T(8,128)(2,1)} async-done(((bf16[64,1024]{1,0:T(8,128)(2,1)}), bf16[1024,1024]{1,0:T(8,128)(2,1)}) %all-gather.5.cloned.1.call-update) | async-done | bytes 2097168 | tf_op jit(solution)/shard_map/all_gather | solution.py:117
  104.5 8.7 %all-to-all-done = bf16[136,16,640]{2,0,1:T(8,128)(2,1)} async-done(((bf16[136,16,640]{2,0,1:T(8,128)(2,1)}), bf16[136,16,640]{2,0,1:T(8,128)(2,1)}, u32[]{:S(2)}, u32[]{:S(2)}) %all-to-all-start) | async-done | bytes 2785312 | tf_op jit(solution)/shard_map/all_to_all | solution.py:73
  113.2 4.2 fusion.65
  117.5 14.5 %reduce-scatter.5.cloned.1.call-done = f32[512,448]{0,1:T(8,128)} async-done(((f32[1024,448]{0,1:T(8,128)}), f32[512,448]{0,1:T(8,128)}) %reduce-scatter.5.cloned.1.call-update) | async-done | bytes 917520 | tf_op jit(solution)/shard_map/reduce_scatter | solution.py:120
  132.0 2.5 copy.80
  134.6 39.8 %reduce-scatter.7.cloned.1.call-done = f32[64,448]{1,0:T(8,128)} async-done(((f32[512,448]{1,0:T(8,128)}), f32[64,448]{1,0:T(8,128)}) %reduce-scatter.7.cloned.1.call-update) | async-done | bytes 114704 | tf_op jit(solution)/shard_map/reduce_scatter | solution.py:121
  174.4 1.5 add_convert_fusion
  177.2 124.9 %all-gather.7.cloned.1.call-done = bf16[16384,448]{1,0:T(8,128)(2,1)} async-done(((bf16[64,448]{1,0:T(8,128)(2,1)}), bf16[16384,448]{1,0:T(8,128)(2,1)}) %all-gather.7.cloned.1.call-update) | async-done | bytes 14680080 | tf_op jit(solution)/shard_map/all_gather | solution.py:134
  302.0 11.9 %multiply_reduce_fusion = (f32[16,40]{1,0:T(8,128)S(1)}, f32[16,40,16,448]{3,1,2,0:T(8,128)}) fusion(bf16[16,16,64,448]{3,2,1,0:T(8,128)(2,1)} %bitcast.118, s32[16,40]{1,0:T(8,128)S(1)} %get-tuple-element.25, pred[16,40]{1,0:T(8,128)(4,1)S(1)} %slice_compare_fusion), kind=kOutput, calls=%fused_computation.1 | convolution fusion | flops 596458880 | bytes 33035904 | tf_op jit(solution)/shard_map/ncg,ndgk->ncdk/dot_general | solution.py:139
  314.0 13.5 %multiply_convert_fusion = bf16[16,40,16,448]{3,1,2,0:T(8,128)(2,1)} fusion(f32[16,40,16,448]{3,1,2,0:T(8,128)} %get-tuple-element.33, f32[16,448]{1,0:T(8,128)S(1)} %reshape.235, f32[16,40]{1,0:T(8,128)S(1)} %add_rsqrt_fusion), kind=kLoop, calls=%fused_computation | loop fusion | flops 13762560 | bytes 27556352 | tf_op jit(solution)/shard_map/convert_element_type | solution.py:147
  327.5 12.4 %copy.69 = bf16[16,40,16,448]{3,2,1,0:T(8,128)(2,1)} copy(bf16[16,40,16,448]{3,1,2,0:T(8,128)(2,1)} %multiply_convert_fusion) | data formatting | bytes 18350080 | tf_op jit(solution)/shard_map/convert_element_type | solution.py:147
  339.9 18.4 %convert_element_type.97 = bf16[640,7168]{1,0:T(8,128)(2,1)} reshape(bf16[16,40,16,448]{3,2,1,0:T(8,128)(2,1)} %copy.69) | data formatting | bytes 18350080 | tf_op jit(solution)/shard_map/convert_element_type | solution.py:147
  358.3 6.8 %fusion.10 = f32[640,128]{1,0:T(8,128)S(1)} fusion(bf16[640,7168]{1,0:T(8,128)(2,1)} %convert_element_type.97, bf16[1,7168,128]{2,1,0:T(8,128)(2,1)} %param.29), kind=kOutput, calls=%fused_computation.15 | convolution fusion | flops 1174405120 | bytes 11337728 | tf_op jit(solution)/shard_map/dot_general | solution.py:148
  365.5 3.2 fusion.21
  368.7 3.6 slice.56
  372.4 33.6 %all-gather.9.cloned.1.call-done = bf16[10240,128]{1,0:T(8,128)(2,1)} async-done(((bf16[640,128]{1,0:T(8,128)(2,1)}), bf16[10240,128]{1,0:T(8,128)(2,1)}) %all-gather.9.cloned.1.call-update) | async-done | bytes 2621456 | tf_op jit(solution)/shard_map/all_gather | solution.py:151
  406.0 4.4 copy.70
  410.4 3.4 fusion.29
  413.8 3.4 fusion.5
  417.3 1.7 fusion.16
  420.3 24.5 %all_to_all.46 = bf16[16,40,448]{2,1,0:T(8,128)(2,1)} all-to-all(bf16[16,40,448]{2,1,0:T(8,128)(2,1)S(1)} %bitcast.127), channel_id=1, replica_groups=mesh['role'=2,'dp'=16,'tensor'=8] {'role','tensor'}, dimensions={0} | all-to-all | bytes 1146880 | tf_op jit(solution)/shard_map/all_to_all | solution.py:167
  444.8 6.8 %all-to-all-start.3 = ((bf16[16,40,448]{2,1,0:T(8,128)(2,1)}), bf16[16,40,448]{2,1,0:T(8,128)(2,1)S(1)}, u32[]{:S(2)}, u32[]{:S(2)}) async-start(bf16[16,40,448]{2,1,0:T(8,128)(2,1)} %all_to_all.46), calls=%async_computation.4 | async-start | bytes 1310720 | tf_op jit(solution)/shard_map/all_to_all | solution.py:168
  451.7 12.1 %all-to-all-done.3 = bf16[16,40,448]{2,1,0:T(8,128)(2,1)S(1)} async-done(((bf16[16,40,448]{2,1,0:T(8,128)(2,1)}), bf16[16,40,448]{2,1,0:T(8,128)(2,1)S(1)}, u32[]{:S(2)}, u32[]{:S(2)}) %all-to-all-start.3) | async-done | bytes 573472 | tf_op jit(solution)/shard_map/all_to_all | solution.py:168
  (74 shorter events, 12.0 us)
Async XLA Ops:
  6.5 410.7 %copy-start = (bf16[3,1,64,7168]{3,2,1,0:T(8,128)(2,1)S(1)}, bf16[3,1,64,7168]{3,2,1,0:T(8,128)(2,1)}, u32[]{:S(2)}) copy-start(bf16[3,1,64,7168]{3,2,1,0:T(8,128)(2,1)} %param.33) | copy-start | bytes 8257540
  8.9 6.1 %slice-start = ((s8[4718592]{0:T(1024)(128)(4,1)}), s8[4194304]{0:T(1024)(128)(4,1)S(1)}, s32[]{:S(2)}) async-start(s8[4718592]{0:T(1024)(128)(4,1)} %bitcast.120), calls=%async_computation.11 | async-start | bytes 8388608
  10.5 4.4 slice-start.1
  16.8 10.2 %copy-start.7 = (s32[64,8]{0,1:T(8,128)S(1)}, s32[64,8]{0,1:T(8,128)}, u32[]{:S(2)}) copy-start(s32[64,8]{0,1:T(8,128)} %param.26) | copy-start | bytes 6148
  16.8 10.6 %copy-start.10 = (s32[64]{0:T(128)S(1)}, s32[64]{0:T(128)}, u32[]{:S(2)}) copy-start(s32[64]{0:T(128)} %param.28) | copy-start | bytes 772
  18.3 13.4 %copy-start.6 = (bf16[3,1,128,64]{2,3,1,0:T(8,128)(2,1)S(1)}, bf16[3,1,128,64]{2,3,1,0:T(8,128)(2,1)}, u32[]{:S(2)}) copy-start(bf16[3,1,128,64]{2,3,1,0:T(8,128)(2,1)} %param.32) | copy-start | bytes 147460
  18.3 24.8 %all-to-all-start.1 = ((bf16[8,64,512]{2,0,1:T(8,128)(2,1)}), bf16[8,64,512]{2,0,1:T(8,128)(2,1)S(1)}, u32[]{:S(2)}, u32[]{:S(2)}) async-start(bf16[8,64,512]{2,0,1:T(8,128)(2,1)} %copy.65), calls=%async_computation.1 | async-start | bytes 1048576 | tf_op jit(solution)/shard_map/all_to_all | solution.py:110
  31.6 1.5 copy-start.2
  43.0 70.2 %all-to-all-start = ((bf16[136,16,640]{2,0,1:T(8,128)(2,1)}), bf16[136,16,640]{2,0,1:T(8,128)(2,1)}, u32[]{:S(2)}, u32[]{:S(2)}) async-start(bf16[136,16,640]{2,0,1:T(8,128)(2,1)} %copy.63), calls=%async_computation | async-start | bytes 5570560 | tf_op jit(solution)/shard_map/all_to_all | solution.py:73
  50.1 54.4 %all-gather.5.cloned.1.call-start = ((), (), s32[]{:S(2)}) async-start(), calls=%async_computation.6 | async-start | bytes 2228224 | tf_op jit(solution)/shard_map/all_gather | solution.py:117
  52.4 79.7 %reduce-scatter.5.cloned.1.call-start = ((), (), s32[]{:S(2)}) async-start(), calls=%async_computation.7 | async-start | bytes 2752512 | tf_op jit(solution)/shard_map/reduce_scatter | solution.py:120
  117.4 56.9 %copy-start.5 = (bf16[64,448]{1,0:T(8,128)(2,1)S(1)}, bf16[64,448]{1,0:T(8,128)(2,1)}, u32[]{:S(2)}) copy-start(bf16[64,448]{1,0:T(8,128)(2,1)} %param.24) | copy-start | bytes 172036
  117.4 58.7 %copy-start.8 = (bf16[7168]{0:T(1024)(128)(2,1)S(1)}, bf16[7168]{0:T(1024)(128)(2,1)}, u32[]{:S(2)}) copy-start(bf16[7168]{0:T(1024)(128)(2,1)} %param.25) | copy-start | bytes 43012
  117.5 56.9 %reduce-scatter.7.cloned.1.call-start = ((), (), s32[]{:S(2)}) async-start(), calls=%async_computation.10 | async-start | bytes 1179648 | tf_op jit(solution)/shard_map/reduce_scatter | solution.py:121
  134.5 167.5 %all-gather.7.cloned.1.call-start = ((), (), s32[]{:S(2)}) async-start(), calls=%async_computation.8 | async-start | bytes 16842752 | tf_op jit(solution)/shard_map/all_gather | solution.py:134
  175.9 230.1 %all-gather.9.cloned.1.call-start = ((), (), s32[]{:S(2)}) async-start(), calls=%async_computation.9 | async-start | bytes 2785280 | tf_op jit(solution)/shard_map/all_gather | solution.py:151
  358.3 6.8 %copy-start.1 = (bf16[640,7168]{1,0:T(8,128)(2,1)S(1)}, bf16[640,7168]{1,0:T(8,128)(2,1)}, u32[]{:S(2)}) copy-start(bf16[640,7168]{1,0:T(8,128)(2,1)} %convert_element_type.97) | copy-start | bytes 27525124
  358.3 7.2 %copy-start.11 = (bf16[1,7168,128]{2,1,0:T(8,128)(2,1)S(1)}, bf16[1,7168,128]{2,1,0:T(8,128)(2,1)}, u32[]{:S(2)}) copy-start(bf16[1,7168,128]{2,1,0:T(8,128)(2,1)} %param.30) | copy-start | bytes 5505028
  410.4 3.4 copy-start.3
  417.2 34.4 %copy-start.9 = (f32[64,8]{0,1:T(8,128)S(1)}, f32[64,8]{0,1:T(8,128)}, u32[]{:S(2)}) copy-start(f32[64,8]{0,1:T(8,128)} %param.27) | copy-start | bytes 6148
  417.2 46.6 %copy-start.4 = (bf16[64,448]{1,0:T(8,128)(2,1)S(1)}, bf16[64,448]{1,0:T(8,128)(2,1)}, u32[]{:S(2)}) copy-start(bf16[64,448]{1,0:T(8,128)(2,1)} %add_convert_fusion) | copy-start | bytes 172036
  444.8 19.0 %all-to-all-start.3 = ((bf16[16,40,448]{2,1,0:T(8,128)(2,1)}), bf16[16,40,448]{2,1,0:T(8,128)(2,1)S(1)}, u32[]{:S(2)}, u32[]{:S(2)}) async-start(bf16[16,40,448]{2,1,0:T(8,128)(2,1)} %all_to_all.46), calls=%async_computation.4 | async-start | bytes 1310720 | tf_op jit(solution)/shard_map/all_to_all | solution.py:168
Sparse Core Ops, SparseCore 0:
  53.3 51.1 all-gather.4
  117.6 14.4 reduce-scatter.4
  134.7 39.6 reduce-scatter.6
  177.8 124.1 all-gather.6
  368.8 37.1 all-gather.8
where the time goes:
time: 473 us; the launch traced here: 471 us
  waiting for transfers between devices  286 us (60%)
  local copies, waits for them, and re-layouts  58.4 us (12%)
  matrix products  44.8 us (9%)
  blocking collectives  24.5 us (5%)
  starting transfers between devices  22.9 us (5%)
  other arithmetic  21.3 us (5%)
  between operations  13.4 us (3%)
    all_gather x1, waiting for transfers between devices, local(): lax.all_gather(mixed_in, ('role', 'tensor', 'dp'), axis=0, tiled=True)  125 us
    all_gather x1, waiting for transfers between devices, local(): all_values = lax.all_gather(head_values, 'dp', axis=0, tiled=True)  52.1 us
    reduce_scatter x1, waiting for transfers between devices, local(): lax.psum_scatter(partial, 'tensor', scatter_dimension=0, tiled=True)  39.8 us
    all_gather x1, waiting for transfers between devices, local(): gathered = lax.all_gather(hidden, RT, axis=0, tiled=False)  33.6 us
    convert_element_type x2, local copies, waits for them, and re-layouts, local(): (picked * scale * norm_gain.astype(jnp.float32)).astype(jnp.bfloat16)  30.8 us
    all_to_all x1, blocking collectives, local(): lax.all_to_all(expert_out, RT, split_axis=0, concat_axis=0, tiled=True)  24.5 us
    reduce_scatter x1, waiting for transfers between devices, local(): partial = lax.psum_scatter(partial, 'role', scatter_dimension=0, tiled=True)  14.5 us
    convert_element_type x1, other arithmetic, local(): (picked * scale * norm_gain.astype(jnp.float32)).astype(jnp.bfloat16)  13.5 us
  transfers between devices with their start and end apart: 8, of which 8 were waited for; matrix products, arithmetic and copies ran while one was open for 5% of the time, Pallas kernels for 0%

commit v1 on v0

--- a/solution.py
+++ b/solution.py
@@ -10,6 +10,12 @@
 NORM_EPS = 1e-06
 MASKED = -1e30
 RT = ("role", "tensor")
+
+
+def joined_along(pieces, dim):
+    pieces = jnp.moveaxis(pieces, 0, dim)
+    shape = pieces.shape
+    return pieces.reshape(*shape[:dim], shape[dim] * shape[dim + 1], *shape[dim + 2 :])
 
 
 def rms_rows(input_rows, norm_gain):
@@ -114,7 +120,19 @@
     head_values = head_values.reshape(
         head_values.shape[0], head_values.shape[1] * head_values.shape[2]
     )
-    all_values = lax.all_gather(head_values, "dp", axis=0, tiled=True)
+    size = lax.axis_size("dp")
+    pairs = [(i, (i + 1) % size) for i in range(size)]
+    back = [(b, a) for a, b in pairs]
+    lower, upper = ([], [])
+    for step in range(size - 1):
+        if step % 2 == 0:
+            lower.append(lax.ppermute(lower[-1] if lower else head_values, "dp", pairs))
+        else:
+            upper.append(lax.ppermute(upper[-1] if upper else head_values, "dp", back))
+    parts = jnp.stack([*lower[::-1], head_values, *upper])
+    shift = lax.axis_index("dp") - len(lower)
+    parts = parts[(jnp.arange(size) - shift) % size]
+    all_values = joined_along(parts, 0)
     down_pack, all_values = lax.optimization_barrier((down_pack, all_values))
     partial = jnp.dot(all_values, out_proj, preferred_element_type=jnp.float32)
     partial = lax.psum_scatter(partial, "role", scatter_dimension=0, tiled=True)

time: 473 us -> 507 us (1.072); the launches traced: 471 us -> 497 us
  starting transfers between devices: 22.9 us -> 62.4 us
  waiting for transfers between devices: 286 us -> 249 us
  local copies, waits for them, and re-layouts: 58.4 us -> 81.2 us
    all_gather x1 -> x0, waiting for transfers between devices: 52.1 us -> none  [local(): all_values = lax.all_gather(head_values, 'dp', axis=0, tiled=True)]
    ppermute x0 -> x15, starting transfers between devices: none -> 39.5 us  [the longest x7 37.4 us: local(): upper.append(lax.ppermute(upper[-1] if upper else head_values, 'dp', back))]
    ppermute x0 -> x15, waiting for transfers between devices: none -> 26.5 us  [the longest x8 26.5 us: local(): lower.append(lax.ppermute(lower[-1] if lower else head_values, 'dp', pairs))]
    unnamed x31 -> x64, local copies, waits for them, and re-layouts: 7.95 us -> 26.5 us
    all_to_all x1, waiting for transfers between devices: 8.75 us -> 0.01 us  [local(): lax.all_to_all(down_pack, RT, split_axis=1, concat_axis=0, tiled=True)]
  transfers between devices with their start and end apart: 8 -> 22, of which waited for: 8 -> 14; matrix products, arithmetic and copies ran while one was open for 5% -> 9% of each run, Pallas kernels for 0% -> 0%
where the time goes in v1:
time: 507 us; the launch traced here: 497 us
  waiting for transfers between devices  249 us (49%)
  local copies, waits for them, and re-layouts  81.2 us (16%)
  starting transfers between devices  62.4 us (12%)
  matrix products  44.9 us (9%)
  blocking collectives  24.5 us (5%)
  other arithmetic  22 us (4%)
  between operations  13.8 us (3%)
    all_gather x1, waiting for transfers between devices, local(): lax.all_gather(mixed_in, ('role', 'tensor', 'dp'), axis=0, tiled=True)  125 us
    reduce_scatter x1, waiting for transfers between devices, local(): lax.psum_scatter(partial, 'tensor', scatter_dimension=0, tiled=True)  39.8 us
    ppermute x7, starting transfers between devices, local(): upper.append(lax.ppermute(upper[-1] if upper else head_values, 'dp', back))  37.4 us
    all_gather x1, waiting for transfers between devices, local(): gathered = lax.all_gather(hidden, RT, axis=0, tiled=False)  33.5 us
    convert_element_type x2, local copies, waits for them, and re-layouts, local(): (picked * scale * norm_gain.astype(jnp.float32)).astype(jnp.bfloat16)  30.8 us
    ppermute x8, waiting for transfers between devices, local(): lower.append(lax.ppermute(lower[-1] if lower else head_values, 'dp', pairs))  26.5 us
    unnamed x64, local copies, waits for them, and re-layouts  26.5 us
    all_to_all x1, blocking collectives, local(): lax.all_to_all(expert_out, RT, split_axis=0, concat_axis=0, tiled=True)  24.5 us
  transfers between devices with their start and end apart: 22, of which 14 were waited for; matrix products, arithmetic and copies ran while one was open for 9% of the time, Pallas kernels for 0%

profile of v1, /device:TPU:32, one launch (start us, length us, event | category | flops | bytes accessed | tf_op | source)
XLA Modules:
  0.0 497.4 jit_solution(2604167252119899325)
XLA Ops:
  10.5 3.8 fusion.7
  18.3 8.6 %all-to-all-start.1 = ((bf16[8,64,512]{2,0,1:T(8,128)(2,1)}), bf16[8,64,512]{2,0,1:T(8,128)(2,1)S(1)}, u32[]{:S(2)}, u32[]{:S(2)}) async-start(bf16[8,64,512]{2,0,1:T(8,128)(2,1)} %copy.67), calls=%async_computation.1 | async-start | bytes 1048576 | tf_op jit(solution)/shard_map/all_to_all | solution.py:116
  27.6 3.9 copy.63
  33.0 3.5 pad_maximum_fusion
  36.5 6.3 %copy.65 = bf16[136,16,640]{2,0,1:T(8,128)(2,1)} copy(bf16[136,16,640]{0,2,1:T(8,128)(2,1)} %pad_maximum_fusion) | data formatting | bytes 5570560 | tf_op jit(solution)/shard_map/concatenate | solution.py:78
  42.9 7.1 %all-to-all-start = ((bf16[136,16,640]{2,0,1:T(8,128)(2,1)}), bf16[136,16,640]{2,0,1:T(8,128)(2,1)}, u32[]{:S(2)}, u32[]{:S(2)}) async-start(bf16[136,16,640]{2,0,1:T(8,128)(2,1)} %copy.65), calls=%async_computation | async-start | bytes 5570560 | tf_op jit(solution)/shard_map/all_to_all | solution.py:79
  53.3 7.4 %collective-permute-done = bf16[64,1024]{1,0:T(8,128)(2,1)S(1)} collective-permute-done((bf16[64,1024]{1,0:T(8,128)(2,1)S(1)}, bf16[64,1024]{1,0:T(8,128)(2,1)S(1)}, u32[]{:S(2)}, u32[]{:S(2)}) %collective-permute-start) | collective-permute-done | bytes 131104 | tf_op jit(solution)/shard_map/ppermute | solution.py:129
  60.7 5.3 %collective-permute-start.8 = (bf16[64,1024]{1,0:T(8,128)(2,1)S(1)}, bf16[64,1024]{1,0:T(8,128)(2,1)S(1)}, u32[]{:S(2)}, u32[]{:S(2)}) collective-permute-start(bf16[64,1024]{1,0:T(8,128)(2,1)S(1)} %copy_bitcast_fusion), channel_id=1, source_target_pairs={{8,0},{16,8},{24,16},{32,24},{40,32},{48,40},{56,48},{64,56},{72,6... | collective-permute-start | bytes 393224 | tf_op jit(solution)/shard_map/ppermute | solution.py:131
  69.0 5.3 %collective-permute-start.9 = (bf16[64,1024]{1,0:T(8,128)(2,1)S(1)}, bf16[64,1024]{1,0:T(8,128)(2,1)S(1)}, u32[]{:S(2)}, u32[]{:S(2)}) collective-permute-start(bf16[64,1024]{1,0:T(8,128)(2,1)S(1)} %collective-permute-done.8), channel_id=1, source_target_pairs={{8,0},{16,8},{24,16},{32,24},{40,32},{48,40},{56,48},{64,56},{72,6... | collective-permute-start | bytes 393224 | tf_op jit(solution)/shard_map/ppermute | solution.py:131
  78.0 5.3 %collective-permute-start.10 = (bf16[64,1024]{1,0:T(8,128)(2,1)S(1)}, bf16[64,1024]{1,0:T(8,128)(2,1)S(1)}, u32[]{:S(2)}, u32[]{:S(2)}) collective-permute-start(bf16[64,1024]{1,0:T(8,128)(2,1)S(1)} %collective-permute-done.9), channel_id=1, source_target_pairs={{8,0},{16,8},{24,16},{32,24},{40,32},{48,40},{56,48},{64,56},{72,6... | collective-permute-start | bytes 393224 | tf_op jit(solution)/shard_map/ppermute | solution.py:131
  86.1 5.5 %collective-permute-start.11 = (bf16[64,1024]{1,0:T(8,128)(2,1)S(1)}, bf16[64,1024]{1,0:T(8,128)(2,1)S(1)}, u32[]{:S(2)}, u32[]{:S(2)}) collective-permute-start(bf16[64,1024]{1,0:T(8,128)(2,1)S(1)} %collective-permute-done.10), channel_id=1, source_target_pairs={{8,0},{16,8},{24,16},{32,24},{40,32},{48,40},{56,48},{64,56},{72,6... | collective-permute-start | bytes 393224 | tf_op jit(solution)/shard_map/ppermute | solution.py:131
  95.0 4.9 collective-permute-start.12
  102.7 5.6 %collective-permute-start.13 = (bf16[64,1024]{1,0:T(8,128)(2,1)}, bf16[64,1024]{1,0:T(8,128)(2,1)}, u32[]{:S(2)}, u32[]{:S(2)}) collective-permute-start(bf16[64,1024]{1,0:T(8,128)(2,1)} %collective-permute-done.12), channel_id=1, source_target_pairs={{8,0},{16,8},{24,16},{32,24},{40,32},{48,40},{56,48},{64,56},{72,6... | collective-permute-start | bytes 393224 | tf_op jit(solution)/shard_map/ppermute | solution.py:131
  112.1 5.4 %collective-permute-start.14 = (bf16[64,1024]{1,0:T(8,128)(2,1)}, bf16[64,1024]{1,0:T(8,128)(2,1)S(1)}, u32[]{:S(2)}, u32[]{:S(2)}) collective-permute-start(bf16[64,1024]{1,0:T(8,128)(2,1)} %collective-permute-done.13), channel_id=1, source_target_pairs={{8,0},{16,8},{24,16},{32,24},{40,32},{48,40},{56,48},{64,56},{72,6... | collective-permute-start | bytes 393224 | tf_op jit(solution)/shard_map/ppermute | solution.py:131
  137.7 3.7 gather_fusion
  141.4 4.2 fusion.66
  145.7 11.5 %reduce-scatter.5.cloned.1.call-done = f32[512,448]{0,1:T(8,128)} async-done(((f32[1024,448]{0,1:T(8,128)}), f32[512,448]{0,1:T(8,128)}) %reduce-scatter.5.cloned.1.call-update) | async-done | bytes 917520 | tf_op jit(solution)/shard_map/reduce_scatter | solution.py:138
  159.8 39.8 %reduce-scatter.7.cloned.1.call-done = f32[64,448]{1,0:T(8,128)} async-done(((f32[512,448]{1,0:T(8,128)}), f32[64,448]{1,0:T(8,128)}) %reduce-scatter.7.cloned.1.call-update) | async-done | bytes 114704 | tf_op jit(solution)/shard_map/reduce_scatter | solution.py:139
  202.4 125.0 %all-gather.4.cloned.1.call-done = bf16[16384,448]{1,0:T(8,128)(2,1)} async-done(((bf16[64,448]{1,0:T(8,128)(2,1)}), bf16[16384,448]{1,0:T(8,128)(2,1)}) %all-gather.4.cloned.1.call-update) | async-done | bytes 14680080 | tf_op jit(solution)/shard_map/all_gather | solution.py:152
  327.4 12.0 %multiply_reduce_fusion = (f32[16,40]{1,0:T(8,128)S(1)}, f32[16,40,16,448]{3,1,2,0:T(8,128)}) fusion(bf16[16,16,64,448]{3,2,1,0:T(8,128)(2,1)} %bitcast.151, s32[16,40]{1,0:T(8,128)S(1)} %get-tuple-element.25, pred[16,40]{1,0:T(8,128)(4,1)S(1)} %slice_compare_fusion), kind=kOutput, calls=%fused_computation.2 | convolution fusion | flops 596458880 | bytes 33035904 | tf_op jit(solution)/shard_map/ncg,ndgk->ncdk/dot_general | solution.py:157
  339.4 13.5 %multiply_convert_fusion = bf16[16,40,16,448]{3,1,2,0:T(8,128)(2,1)} fusion(f32[16,40,16,448]{3,1,2,0:T(8,128)} %get-tuple-element.33, f32[16,448]{1,0:T(8,128)S(1)} %reshape.288, f32[16,40]{1,0:T(8,128)S(1)} %add_rsqrt_fusion), kind=kLoop, calls=%fused_computation.1 | loop fusion | flops 13762560 | bytes 27556352 | tf_op jit(solution)/shard_map/convert_element_type | solution.py:165
  352.9 12.4 %copy.72 = bf16[16,40,16,448]{3,2,1,0:T(8,128)(2,1)} copy(bf16[16,40,16,448]{3,1,2,0:T(8,128)(2,1)} %multiply_convert_fusion) | data formatting | bytes 18350080 | tf_op jit(solution)/shard_map/convert_element_type | solution.py:165
  365.4 18.4 %convert_element_type.97 = bf16[640,7168]{1,0:T(8,128)(2,1)} reshape(bf16[16,40,16,448]{3,2,1,0:T(8,128)(2,1)} %copy.72) | data formatting | bytes 18350080 | tf_op jit(solution)/shard_map/convert_element_type | solution.py:165
  383.8 6.8 %fusion.10 = f32[640,128]{1,0:T(8,128)S(1)} fusion(bf16[640,7168]{1,0:T(8,128)(2,1)} %convert_element_type.97, bf16[1,7168,128]{2,1,0:T(8,128)(2,1)} %param.29), kind=kOutput, calls=%fused_computation.16 | convolution fusion | flops 1174405120 | bytes 11337728 | tf_op jit(solution)/shard_map/dot_general | solution.py:166
  394.2 3.6 slice.58
  398.0 33.5 %all-gather.6.cloned.1.call-done = bf16[10240,128]{1,0:T(8,128)(2,1)} async-done(((bf16[640,128]{1,0:T(8,128)(2,1)}), bf16[10240,128]{1,0:T(8,128)(2,1)}) %all-gather.6.cloned.1.call-update) | async-done | bytes 2621456 | tf_op jit(solution)/shard_map/all_gather | solution.py:169
  431.5 4.6 copy.73
  436.1 3.4 fusion.28
  439.5 3.4 fusion.5
  446.0 24.5 %all_to_all.46 = bf16[16,40,448]{2,1,0:T(8,128)(2,1)} all-to-all(bf16[16,40,448]{2,1,0:T(8,128)(2,1)S(1)} %bitcast.160), channel_id=1, replica_groups=mesh['role'=2,'dp'=16,'tensor'=8] {'role','tensor'}, dimensions={0} | all-to-all | bytes 1146880 | tf_op jit(solution)/shard_map/all_to_all | solution.py:185
  470.5 6.8 %all-to-all-start.3 = ((bf16[16,40,448]{2,1,0:T(8,128)(2,1)}), bf16[16,40,448]{2,1,0:T(8,128)(2,1)S(1)}, u32[]{:S(2)}, u32[]{:S(2)}) async-start(bf16[16,40,448]{2,1,0:T(8,128)(2,1)} %all_to_all.46), calls=%async_computation.4 | async-start | bytes 1310720 | tf_op jit(solution)/shard_map/all_to_all | solution.py:186
  477.4 12.1 %all-to-all-done.3 = bf16[16,40,448]{2,1,0:T(8,128)(2,1)S(1)} async-done(((bf16[16,40,448]{2,1,0:T(8,128)(2,1)}), bf16[16,40,448]{2,1,0:T(8,128)(2,1)S(1)}, u32[]{:S(2)}, u32[]{:S(2)}) %all-to-all-start.3) | async-done | bytes 573472 | tf_op jit(solution)/shard_map/all_to_all | solution.py:186
  (140 shorter events, 66.3 us)
Async XLA Ops:
  6.5 436.4 %copy-start = (bf16[3,1,64,7168]{3,2,1,0:T(8,128)(2,1)S(1)}, bf16[3,1,64,7168]{3,2,1,0:T(8,128)(2,1)}, u32[]{:S(2)}) copy-start(bf16[3,1,64,7168]{3,2,1,0:T(8,128)(2,1)} %param.33) | copy-start | bytes 8257540
  18.3 24.6 %all-to-all-start.1 = ((bf16[8,64,512]{2,0,1:T(8,128)(2,1)}), bf16[8,64,512]{2,0,1:T(8,128)(2,1)S(1)}, u32[]{:S(2)}, u32[]{:S(2)}) async-start(bf16[8,64,512]{2,0,1:T(8,128)(2,1)} %copy.67), calls=%async_computation.1 | async-start | bytes 1048576 | tf_op jit(solution)/shard_map/all_to_all | solution.py:116
  42.9 98.5 %all-to-all-start = ((bf16[136,16,640]{2,0,1:T(8,128)(2,1)}), bf16[136,16,640]{2,0,1:T(8,128)(2,1)}, u32[]{:S(2)}, u32[]{:S(2)}) async-start(bf16[136,16,640]{2,0,1:T(8,128)(2,1)} %copy.65), calls=%async_computation | async-start | bytes 5570560 | tf_op jit(solution)/shard_map/all_to_all | solution.py:79
  50.0 107.2 %reduce-scatter.5.cloned.1.call-start = ((), (), s32[]{:S(2)}) async-start(), calls=%async_computation.6 | async-start | bytes 2752512 | tf_op jit(solution)/shard_map/reduce_scatter | solution.py:138
  51.6 9.1 %collective-permute-start = (bf16[64,1024]{1,0:T(8,128)(2,1)S(1)}, bf16[64,1024]{1,0:T(8,128)(2,1)S(1)}, u32[]{:S(2)}, u32[]{:S(2)}) collective-permute-start(bf16[64,1024]{1,0:T(8,128)(2,1)S(1)} %copy_bitcast_fusion), channel_id=1, source_target_pairs={{0,8},{8,16},{16,24},{24,32},{32,40},{40,48},{48,56},{56,64},{64,7... | collective-permute-start | bytes 393224 | tf_op jit(solution)/shard_map/ppermute | solution.py:129
  60.7 8.3 %collective-permute-start.1 = (bf16[64,1024]{1,0:T(8,128)(2,1)S(1)}, bf16[64,1024]{1,0:T(8,128)(2,1)S(1)}, u32[]{:S(2)}, u32[]{:S(2)}) collective-permute-start(bf16[64,1024]{1,0:T(8,128)(2,1)S(1)} %collective-permute-done), channel_id=1, source_target_pairs={{0,8},{8,16},{16,24},{24,32},{32,40},{40,48},{48,56},{56,64},{64,7... | collective-permute-start | bytes 393224 | tf_op jit(solution)/shard_map/ppermute | solution.py:129
  60.7 8.3 %collective-permute-start.8 = (bf16[64,1024]{1,0:T(8,128)(2,1)S(1)}, bf16[64,1024]{1,0:T(8,128)(2,1)S(1)}, u32[]{:S(2)}, u32[]{:S(2)}) collective-permute-start(bf16[64,1024]{1,0:T(8,128)(2,1)S(1)} %copy_bitcast_fusion), channel_id=1, source_target_pairs={{8,0},{16,8},{24,16},{32,24},{40,32},{48,40},{56,48},{64,56},{72,6... | collective-permute-start | bytes 393224 | tf_op jit(solution)/shard_map/ppermute | solution.py:131
  69.0 8.3 %collective-permute-start.2 = (bf16[64,1024]{1,0:T(8,128)(2,1)S(1)}, bf16[64,1024]{1,0:T(8,128)(2,1)S(1)}, u32[]{:S(2)}, u32[]{:S(2)}) collective-permute-start(bf16[64,1024]{1,0:T(8,128)(2,1)S(1)} %collective-permute-done.1), channel_id=1, source_target_pairs={{0,8},{8,16},{16,24},{24,32},{32,40},{40,48},{48,56},{56,64},{64,7... | collective-permute-start | bytes 393224 | tf_op jit(solution)/shard_map/ppermute | solution.py:129
  69.0 8.3 %collective-permute-start.9 = (bf16[64,1024]{1,0:T(8,128)(2,1)S(1)}, bf16[64,1024]{1,0:T(8,128)(2,1)S(1)}, u32[]{:S(2)}, u32[]{:S(2)}) collective-permute-start(bf16[64,1024]{1,0:T(8,128)(2,1)S(1)} %collective-permute-done.8), channel_id=1, source_target_pairs={{8,0},{16,8},{24,16},{32,24},{40,32},{48,40},{56,48},{64,56},{72,6... | collective-permute-start | bytes 393224 | tf_op jit(solution)/shard_map/ppermute | solution.py:131
  77.3 8.3 %collective-permute-start.3 = (bf16[64,1024]{1,0:T(8,128)(2,1)S(1)}, bf16[64,1024]{1,0:T(8,128)(2,1)S(1)}, u32[]{:S(2)}, u32[]{:S(2)}) collective-permute-start(bf16[64,1024]{1,0:T(8,128)(2,1)S(1)} %collective-permute-done.2), channel_id=1, source_target_pairs={{0,8},{8,16},{16,24},{24,32},{32,40},{40,48},{48,56},{56,64},{64,7... | collective-permute-start | bytes 393224 | tf_op jit(solution)/shard_map/ppermute | solution.py:129
  78.0 8.0 %collective-permute-start.10 = (bf16[64,1024]{1,0:T(8,128)(2,1)S(1)}, bf16[64,1024]{1,0:T(8,128)(2,1)S(1)}, u32[]{:S(2)}, u32[]{:S(2)}) collective-permute-start(bf16[64,1024]{1,0:T(8,128)(2,1)S(1)} %collective-permute-done.9), channel_id=1, source_target_pairs={{8,0},{16,8},{24,16},{32,24},{40,32},{48,40},{56,48},{64,56},{72,6... | collective-permute-start | bytes 393224 | tf_op jit(solution)/shard_map/ppermute | solution.py:131
  85.6 26.4 %copy-start.12 = (bf16[64,1024]{1,0:T(8,128)(2,1)}, bf16[64,1024]{1,0:T(8,128)(2,1)S(1)}, u32[]{:S(2)}) copy-start(bf16[64,1024]{1,0:T(8,128)(2,1)S(1)} %collective-permute-done.3) | copy-start | bytes 393220
  85.6 8.7 %collective-permute-start.4 = (bf16[64,1024]{1,0:T(8,128)(2,1)S(1)}, bf16[64,1024]{1,0:T(8,128)(2,1)S(1)}, u32[]{:S(2)}, u32[]{:S(2)}) collective-permute-start(bf16[64,1024]{1,0:T(8,128)(2,1)S(1)} %collective-permute-done.3), channel_id=1, source_target_pairs={{0,8},{8,16},{16,24},{24,32},{32,40},{40,48},{48,56},{56,64},{64,7... | collective-permute-start | bytes 393224 | tf_op jit(solution)/shard_map/ppermute | solution.py:129
  86.1 8.3 %collective-permute-start.11 = (bf16[64,1024]{1,0:T(8,128)(2,1)S(1)}, bf16[64,1024]{1,0:T(8,128)(2,1)S(1)}, u32[]{:S(2)}, u32[]{:S(2)}) collective-permute-start(bf16[64,1024]{1,0:T(8,128)(2,1)S(1)} %collective-permute-done.10), channel_id=1, source_target_pairs={{8,0},{16,8},{24,16},{32,24},{40,32},{48,40},{56,48},{64,56},{72,6... | collective-permute-start | bytes 393224 | tf_op jit(solution)/shard_map/ppermute | solution.py:131
  94.3 8.4 %collective-permute-start.5 = (bf16[64,1024]{1,0:T(8,128)(2,1)S(1)}, bf16[64,1024]{1,0:T(8,128)(2,1)}, u32[]{:S(2)}, u32[]{:S(2)}) collective-permute-start(bf16[64,1024]{1,0:T(8,128)(2,1)S(1)} %collective-permute-done.4), channel_id=1, source_target_pairs={{0,8},{8,16},{16,24},{24,32},{32,40},{40,48},{48,56},{56,64},{64,7... | collective-permute-start | bytes 393224 | tf_op jit(solution)/shard_map/ppermute | solution.py:129
  95.0 17.0 %copy-start.10 = (bf16[64,1024]{1,0:T(8,128)(2,1)}, bf16[64,1024]{1,0:T(8,128)(2,1)S(1)}, u32[]{:S(2)}) copy-start(bf16[64,1024]{1,0:T(8,128)(2,1)S(1)} %collective-permute-done.11) | copy-start | bytes 393220
  95.0 7.7 %collective-permute-start.12 = (bf16[64,1024]{1,0:T(8,128)(2,1)S(1)}, bf16[64,1024]{1,0:T(8,128)(2,1)}, u32[]{:S(2)}, u32[]{:S(2)}) collective-permute-start(bf16[64,1024]{1,0:T(8,128)(2,1)S(1)} %collective-permute-done.11), channel_id=1, source_target_pairs={{8,0},{16,8},{24,16},{32,24},{40,32},{48,40},{56,48},{64,56},{72,6... | collective-permute-start | bytes 393224 | tf_op jit(solution)/shard_map/ppermute | solution.py:131
  102.7 8.6 %collective-permute-start.6 = (bf16[64,1024]{1,0:T(8,128)(2,1)}, bf16[64,1024]{1,0:T(8,128)(2,1)}, u32[]{:S(2)}, u32[]{:S(2)}) collective-permute-start(bf16[64,1024]{1,0:T(8,128)(2,1)} %collective-permute-done.5), channel_id=1, source_target_pairs={{0,8},{8,16},{16,24},{24,32},{32,40},{40,48},{48,56},{56,64},{64,7... | collective-permute-start | bytes 393224 | tf_op jit(solution)/shard_map/ppermute | solution.py:129
  102.7 9.4 %collective-permute-start.13 = (bf16[64,1024]{1,0:T(8,128)(2,1)}, bf16[64,1024]{1,0:T(8,128)(2,1)}, u32[]{:S(2)}, u32[]{:S(2)}) collective-permute-start(bf16[64,1024]{1,0:T(8,128)(2,1)} %collective-permute-done.12), channel_id=1, source_target_pairs={{8,0},{16,8},{24,16},{32,24},{40,32},{48,40},{56,48},{64,56},{72,6... | collective-permute-start | bytes 393224 | tf_op jit(solution)/shard_map/ppermute | solution.py:131
  111.3 8.6 %collective-permute-start.7 = (bf16[64,1024]{1,0:T(8,128)(2,1)}, bf16[64,1024]{1,0:T(8,128)(2,1)}, u32[]{:S(2)}, u32[]{:S(2)}) collective-permute-start(bf16[64,1024]{1,0:T(8,128)(2,1)} %collective-permute-done.6), channel_id=1, source_target_pairs={{0,8},{8,16},{16,24},{24,32},{32,40},{40,48},{48,56},{56,64},{64,7... | collective-permute-start | bytes 393224 | tf_op jit(solution)/shard_map/ppermute | solution.py:129
  112.0 19.9 %copy-start.6 = (bf16[64,1024]{1,0:T(8,128)(2,1)S(1)}, bf16[64,1024]{1,0:T(8,128)(2,1)}, u32[]{:S(2)}) copy-start(bf16[64,1024]{1,0:T(8,128)(2,1)} %copy-done.5) | copy-start | bytes 393220
  112.1 20.5 %copy-start.9 = (bf16[64,1024]{1,0:T(8,128)(2,1)S(1)}, bf16[64,1024]{1,0:T(8,128)(2,1)}, u32[]{:S(2)}) copy-start(bf16[64,1024]{1,0:T(8,128)(2,1)} %copy-done.8) | copy-start | bytes 393220
  112.1 21.2 %copy-start.11 = (bf16[64,1024]{1,0:T(8,128)(2,1)S(1)}, bf16[64,1024]{1,0:T(8,128)(2,1)}, u32[]{:S(2)}) copy-start(bf16[64,1024]{1,0:T(8,128)(2,1)} %copy-done.10) | copy-start | bytes 393220
  112.1 24.9 %collective-permute-start.14 = (bf16[64,1024]{1,0:T(8,128)(2,1)}, bf16[64,1024]{1,0:T(8,128)(2,1)S(1)}, u32[]{:S(2)}, u32[]{:S(2)}) collective-permute-start(bf16[64,1024]{1,0:T(8,128)(2,1)} %collective-permute-done.13), channel_id=1, source_target_pairs={{8,0},{16,8},{24,16},{32,24},{40,32},{48,40},{56,48},{64,56},{72,6... | collective-permute-start | bytes 393224 | tf_op jit(solution)/shard_map/ppermute | solution.py:131
  145.7 53.9 %copy-start.14 = (bf16[64,448]{1,0:T(8,128)(2,1)S(1)}, bf16[64,448]{1,0:T(8,128)(2,1)}, u32[]{:S(2)}) copy-start(bf16[64,448]{1,0:T(8,128)(2,1)} %param.24) | copy-start | bytes 172036
  145.7 55.7 %copy-start.17 = (bf16[7168]{0:T(1024)(128)(2,1)S(1)}, bf16[7168]{0:T(1024)(128)(2,1)}, u32[]{:S(2)}) copy-start(bf16[7168]{0:T(1024)(128)(2,1)} %param.25) | copy-start | bytes 43012
  145.7 53.9 %reduce-scatter.7.cloned.1.call-start = ((), (), s32[]{:S(2)}) async-start(), calls=%async_computation.9 | async-start | bytes 1179648 | tf_op jit(solution)/shard_map/reduce_scatter | solution.py:139
  159.8 167.7 %all-gather.4.cloned.1.call-start = ((), (), s32[]{:S(2)}) async-start(), calls=%async_computation.7 | async-start | bytes 16842752 | tf_op jit(solution)/shard_map/all_gather | solution.py:152
  201.2 230.3 %all-gather.6.cloned.1.call-start = ((), (), s32[]{:S(2)}) async-start(), calls=%async_computation.8 | async-start | bytes 2785280 | tf_op jit(solution)/shard_map/all_gather | solution.py:169
  444.7 32.7 %copy-start.18 = (f32[64,8]{0,1:T(8,128)S(1)}, f32[64,8]{0,1:T(8,128)}, u32[]{:S(2)}) copy-start(f32[64,8]{0,1:T(8,128)} %param.27) | copy-start | bytes 6148
  444.7 44.9 %copy-start.4 = (bf16[64,448]{1,0:T(8,128)(2,1)S(1)}, bf16[64,448]{1,0:T(8,128)(2,1)}, u32[]{:S(2)}) copy-start(bf16[64,448]{1,0:T(8,128)(2,1)} %add_convert_fusion) | copy-start | bytes 172036
  470.5 19.0 %all-to-all-start.3 = ((bf16[16,40,448]{2,1,0:T(8,128)(2,1)}), bf16[16,40,448]{2,1,0:T(8,128)(2,1)S(1)}, u32[]{:S(2)}, u32[]{:S(2)}) async-start(bf16[16,40,448]{2,1,0:T(8,128)(2,1)} %all_to_all.46), calls=%async_computation.4 | async-start | bytes 1310720 | tf_op jit(solution)/shard_map/all_to_all | solution.py:186
  (13 other events, 70.0 us)
Sparse Core Ops, SparseCore 0:
  145.8 11.3 reduce-scatter.4
  159.9 39.6 reduce-scatter.6
  203.2 124.1 all-gather.3
  394.3 37.1 all-gather.5
